TPU v7x, 32 devices: a whole 2x2x4 slice. The times are simulated.
32 devices in a mesh: ctx: 8 (over z, y), ch: 4 (over x, core).
Axes of the slice: x: 2, y: 2, z: 4, core: 2. Of those that a mesh axis runs over, the one named last changes fastest.
Arguments:
- projected: bfloat16 [3, 8192, 4096], P(None, 'ctx', 'ch'), may hold values from -6 to 6
- tap_weights: bfloat16 [3, 3, 4096], P(None, None, 'ch'), may hold values from -3.59375 to 3.59375
- pole_rates: float32 [16, 4096], P(None, 'ch'), may hold values from 1.2207031e-05 to 0.0625
- residues: float32 [16, 4096], P(None, 'ch'), may hold values from -1.4143862 to 1.4143862
- long_bias: float32 [4096], P('ch'), may hold values from -4 to 4
- out_weight: bfloat16 [4096, 4096], P(None, 'ch'), may hold values from -0.09375 to 0.09375
Outputs:
- mixed_out: bfloat16 [8192, 4096], P('ctx', 'ch')
All inputs are finite; a program needn't handle non-finite values.
Results may differ from a plain program's by a relative error of at most 0.012.
Values may be sent and summed in bfloat16 or wider, within the bound.
No kernel may reach another device: no remote copies, remote signals or barrier semaphores. Data moves between devices by JAX's collectives and lax.ppermute only.
A program may use at most 256 MiB of HBM per device.

v0:
```python
import jax
import jax.numpy as jnp
from jax import lax
from jax.sharding import PartitionSpec as P

BLOCK = 64


def shifted(value, axis, steps):
    count = lax.axis_size(axis)
    initial, last = (max(0, -steps), min(count, count - steps))
    return lax.ppermute(value, axis, [(source, source + steps) for source in range(initial, last)])


def make_tables(pole_rates, residues, block_size):
    lag_steps = jnp.arange(block_size, dtype=jnp.float32)
    powers = jnp.exp(-pole_rates[None, :, :] * lag_steps[:, None, None])
    kernel = jnp.sum(powers * residues[None, :, :], axis=1)
    offsets = (
        jnp.arange(block_size, dtype=jnp.int32)[:, None]
        - jnp.arange(block_size, dtype=jnp.int32)[None, :]
    )
    toeplitz = jnp.where(
        (offsets >= 0)[:, :, None], kernel[jnp.maximum(offsets, 0)], jnp.float32(0.0)
    )
    end_weights = powers[::-1]
    read_weights = powers * jnp.exp(-pole_rates)[None, :, :] * residues[None, :, :]
    block_decay = jnp.exp(-pole_rates * block_size)
    return (toeplitz, end_weights, read_weights, block_decay)


def combine(earlier, latter):
    return (earlier[0] * latter[0], latter[0] * earlier[1] + latter[1])


def channel_conv(rows_last, pole_rates, residues):
    highest = lax.Precision.HIGHEST
    channel_count = rows_last.shape[0]
    length = rows_last.shape[1]
    block_count = length // BLOCK
    pole_count = pole_rates.shape[0]
    toeplitz, end_weights, read_weights, block_decay = make_tables(pole_rates, residues, BLOCK)
    toeplitz_c = jnp.transpose(toeplitz, (2, 0, 1))
    blocks = rows_last.astype(jnp.float32).reshape(channel_count, block_count, BLOCK)
    inner_part = jnp.einsum("cij,cnj->cni", toeplitz_c, blocks, precision=highest)
    closing = jnp.einsum("jpc,cnj->ncp", end_weights, blocks, precision=highest)
    closing = closing.reshape(block_count, channel_count * pole_count)
    decay_row = jnp.transpose(block_decay).reshape(1, channel_count * pole_count)
    decays = jnp.broadcast_to(decay_row, closing.shape)
    _, states = lax.associative_scan(combine, (decays, closing), axis=0)
    before_state = jnp.concatenate([jnp.zeros_like(states[:1]), states[:-1]], 0)
    before_state = before_state.reshape(block_count, channel_count, pole_count)
    carried = jnp.einsum("ipc,ncp->cni", read_weights, before_state, precision=highest)
    return (inner_part + carried).reshape(channel_count, length)


def shards(projected, tap_weights, pole_rates, residues, long_bias, out_weight):
    row_count = projected.shape[1]
    rim_rows = tap_weights.shape[0] - 1
    prior_rows = shifted(projected[:, row_count - rim_rows :], "ctx", 1)
    extended = jnp.concatenate([prior_rows, projected], 1)
    featured = jnp.zeros(projected.shape, jnp.float32)
    for tap_index in range(rim_rows + 1):
        lead_row = rim_rows - tap_index
        featured = featured + tap_weights[tap_index].astype(jnp.float32)[:, None, :] * extended[
            :, lead_row : lead_row + row_count
        ].astype(jnp.float32)
    mixed_input = (featured[1] * featured[2]).astype(jnp.bfloat16)
    channel_major = jnp.transpose(mixed_input)
    spread = lax.all_to_all(channel_major, "ctx", split_axis=0, concat_axis=1, tiled=True)
    share_width = spread.shape[0]
    first_channel = lax.axis_index("ctx") * share_width
    rates_here = lax.dynamic_slice_in_dim(pole_rates, first_channel, share_width, 1)
    residues_here = lax.dynamic_slice_in_dim(residues, first_channel, share_width, 1)
    long_part = channel_conv(spread, rates_here, residues_here).astype(jnp.bfloat16)
    returned = lax.all_to_all(long_part, "ctx", split_axis=1, concat_axis=0, tiled=True)
    long_mix = jnp.transpose(returned)
    gated_mix = featured[0] * (
        long_mix.astype(jnp.float32) + long_bias[None, :] * mixed_input.astype(jnp.float32)
    )
    gated_mix = gated_mix.astype(jnp.bfloat16)
    mixed_out = jnp.dot(
        lax.all_gather(gated_mix, "ch", axis=1, tiled=True),
        out_weight,
        preferred_element_type=jnp.float32,
    )
    return mixed_out.astype(jnp.bfloat16)


def solution(mesh):
    in_specs = (
        P(None, "ctx", "ch"),
        P(None, None, "ch"),
        P(None, "ch"),
        P(None, "ch"),
        P("ch"),
        P(None, "ch"),
    )
    out_specs = P("ctx", "ch")
    return jax.shard_map(shards, mesh=mesh, in_specs=in_specs, out_specs=out_specs, check_vma=False)
```

profile of v0, /device:TPU:0, one launch (start us, length us, event | category | flops | bytes accessed | tf_op | source)
XLA Modules:
  0.0 405.2 jit_solution(4329657434524788336)
XLA Ops:
  7.4 4.9 %collective-permute-start = (bf16[3,2,1024]{2,1,0:T(2,128)(2,1)S(1)}, bf16[3,2,1024]{2,1,0:T(2,128)(2,1)S(1)}, u32[]{:S(2)}, u32[]{:S(2)}) collective-permute-start(bf16[3,2,1024]{2,1,0:T(2,128)(2,1)S(1)} %slice.176), channel_id=1, source_target_pairs={{0,4},{4,8},{8,12},{12,16},{16,20},{20,24},{24,28},{1,5},{5,9},{9,... | collective-permute-start | bytes 36872 | tf_op jit(solution)/shard_map/ppermute | solution.py:12
  13.0 8.7 %copy.43 = bf16[3,1024,1024]{1,2,0:T(8,128)(2,1)} copy(bf16[3,1024,1024]{2,1,0:T(8,128)(2,1)} %param.6) | data formatting | bytes 12582912 | tf_op args[0]
  22.1 15.7 %multiply_add_fusion = f32[3,1024,1024]{1,2,0:T(8,128)S(1)} fusion(bf16[3,1024,1024]{1,2,0:T(8,128)(2,1)} %copy.43, bf16[3,2,1024]{1,2,0:T(8,128)(2,1)S(1)} %copy.44, f32[3,1024]{1,0:T(4,128)S(1)} %get-tuple-element.12, f32[3,1024]{1,0:T(4,128)S(1)} %get-tuple-element.13, f32[3,1024]{1,0:T(4,128)S(1)} %get-tuple-element.11), kind=kLoop, calls=%fused_computation.1 | loop fusion | flops 44040192 | bytes 18923520 | tf_op jit(solution)/shard_map/add | solution.py:65
  37.8 4.5 %copy-done = f32[3,1024,1024]{1,2,0:T(8,128)} copy-done((f32[3,1024,1024]{1,2,0:T(8,128)}, f32[3,1024,1024]{1,2,0:T(8,128)S(1)}, u32[]{:S(2)}) %copy-start) | copy-done | bytes 12582936
  44.3 4.9 %all-to-all-start = ((bf16[8,128,1024]{2,1,0:T(8,128)(2,1)}), bf16[8,128,1024]{2,1,0:T(8,128)(2,1)}, u32[]{:S(2)}, u32[]{:S(2)}) async-start(bf16[8,128,1024]{2,1,0:T(8,128)(2,1)} %bitcast.6), calls=%async_computation | async-start | bytes 4194304 | tf_op jit(solution)/shard_map/all_to_all | solution.py:70
  53.5 10.8 %gather_fusion = f32[4096,128]{1,0:T(8,128)S(1)} fusion(f32[64,128]{1,0:T(8,128)S(1)} %copy.49, s32[4096]{0:T(1024)S(1)} %broadcast_clamp_fusion), kind=kCustom, calls=%fused_computation | custom fusion | bytes 4210688 | tf_op jit(solution)/shard_map/gather | solution.py:24
  64.3 4.6 %copy.50 = f32[64,64,128]{1,0,2:T(8,128)} copy(f32[64,64,128]{2,1,0:T(8,128)S(1)} %bitcast.56) | data formatting | bytes 4194304 | tf_op jit(solution)/shard_map/gather | solution.py:24
  70.8 26.5 %all-to-all-done = bf16[8,128,1024]{2,1,0:T(8,128)(2,1)} async-done(((bf16[8,128,1024]{2,1,0:T(8,128)(2,1)}), bf16[8,128,1024]{2,1,0:T(8,128)(2,1)}, u32[]{:S(2)}, u32[]{:S(2)}) %all-to-all-start) | async-done | bytes 2097184 | tf_op jit(solution)/shard_map/all_to_all | solution.py:70
  97.3 3.9 copy.46
  101.2 3.8 copy.51
  105.0 3.0 fusion.25
  108.0 20.3 %slice.187 = f32[64,2048]{0,1:T(8,128)} slice(f32[128,2048]{0,1:T(8,128)S(1)} %bitcast.52), slice={[0:127:2], [0:2048:1]} | slice | bytes 1048576 | tf_op jit(solution)/shard_map/slice | solution.py:50
  128.3 21.9 %slice.188 = f32[64,2048]{0,1:T(8,128)} slice(f32[128,2048]{0,1:T(8,128)S(1)} %bitcast.53), slice={[1:128:2], [0:2048:1]} | slice | bytes 1048576 | tf_op jit(solution)/shard_map/slice | solution.py:50
  184.5 21.6 %slice.226 = f32[63,2048]{0,1:T(8,128)} slice(f32[128,2048]{0,1:T(8,128)S(1)} %bitcast.54), slice={[2:128:2], [0:2048:1]} | slice | bytes 1032192 | tf_op jit(solution)/shard_map/slice | solution.py:50
  220.8 2.7 pad.55
  225.6 4.6 %pad.116 = f32[128,2048]{1,0:T(8,128)} pad(f32[64,2048]{1,0:T(8,128)} %add.128, f32[]{:T(128)} %constant.5.clone.1), padding=1_0_1x0_0_0 | pad | bytes 1572868
  243.5 4.2 %fusion.4 = f32[128,128,64]{1,2,0:T(8,128)S(1)} fusion(bf16[128,128,64]{1,2,0:T(8,128)(2,1)S(1)} %copy.51, f32[64,64,128]{1,0,2:T(8,128)} %copy.50, pred[64,64]{1,0:T(8,128)(4,1)S(1)} %copy-done.8), kind=kOutput, calls=%fused_computation.12 | convolution fusion | flops 805830656 | bytes 8392704 | tf_op jit(solution)/shard_map/cij,cnj->cni/dot_general | solution.py:45
  247.7 7.8 %add_convert_fusion = bf16[128,128,64]{1,2,0:T(8,128)(2,1)S(1)} fusion(f32[128,128,64]{1,2,0:T(8,128)S(1)} %fusion.4, f32[128,128,16]{0,2,1:T(8,128)S(1)} %bitcast.59, f32[16,128]{0,1:T(8,128)S(1)} %copy-done.6, f32[16,128]{0,1:T(8,128)S(1)} %copy-done.5, f32[16,128]{0,1:T(8,128)S(1)} %copy-done.3), kind=kOutput, calls=%fused_computation.15 | convolution fusion | flops 203816960 | bytes 7364608 | tf_op jit(solution)/shard_map/ipc,ncp->cni/dot_general | solution.py:53
  255.6 3.3 copy.60
  258.8 52.0 %all_to_all.26 = bf16[128,8,1024]{0,2,1:T(8,128)(2,1)S(1)} all-to-all(bf16[128,8,1024]{0,2,1:T(8,128)(2,1)} %bitcast.58), channel_id=1, replica_groups=mesh['ctx'=8,'ch'=4] {'ctx'}, dimensions={1} | all-to-all | bytes 4194304 | tf_op jit(solution)/shard_map/all_to_all | solution.py:76
  313.1 5.4 %copy.61 = f32[8,128,1024]{2,1,0:T(8,128)} copy(f32[8,128,1024]{1,2,0:T(8,128)} %convert_bitcast_fusion) | data formatting | bytes 8388608 | tf_op jit(solution)/shard_map/convert_element_type | solution.py:79
  318.5 7.7 %fusion.3 = bf16[1024,1024]{0,1:T(8,128)(2,1)} fusion(f32[3,1024,1024]{1,2,0:T(8,128)} %copy-done, f32[8,128,1024]{2,1,0:T(8,128)} %copy.61, f32[1024]{0:T(1024)S(1)} %copy-done.9), kind=kLoop, calls=%fused_computation.10 | loop fusion | flops 7340032 | bytes 18878464 | tf_op jit(solution)/shard_map/convert_element_type | solution.py:81
  326.2 57.5 %all-gather.2.cloned.1.call-done = bf16[1024,4096]{0,1:T(8,128)(2,1)} async-done(((bf16[1024,1024]{0,1:T(8,128)(2,1)}), bf16[1024,4096]{0,1:T(8,128)(2,1)}) %all-gather.2.cloned.1.call-update) | async-done | bytes 8388624 | tf_op jit(solution)/shard_map/all_gather | solution.py:83
  383.7 14.7 %convolution_convert_fusion = bf16[1024,1024]{1,0:T(8,128)(2,1)} fusion(bf16[1024,4096]{0,1:T(8,128)(2,1)} %all-gather.2.cloned.1.call-done, bf16[4096,1024]{1,0:T(8,128)(2,1)} %param.11), kind=kOutput, calls=%fused_computation.19 | convolution fusion | flops 8590983168 | bytes 18874368 | tf_op jit(solution)/shard_map/dot_general | solution.py:82
  (107 shorter events, 76.7 us)
Async XLA Ops:
  7.4 14.3 %collective-permute-start = (bf16[3,2,1024]{2,1,0:T(2,128)(2,1)S(1)}, bf16[3,2,1024]{2,1,0:T(2,128)(2,1)S(1)}, u32[]{:S(2)}, u32[]{:S(2)}) collective-permute-start(bf16[3,2,1024]{2,1,0:T(2,128)(2,1)S(1)} %slice.176), channel_id=1, source_target_pairs={{0,4},{4,8},{8,12},{12,16},{16,20},{20,24},{24,28},{1,5},{5,9},{9,... | collective-permute-start | bytes 36872 | tf_op jit(solution)/shard_map/ppermute | solution.py:12
  37.8 4.5 %copy-start = (f32[3,1024,1024]{1,2,0:T(8,128)}, f32[3,1024,1024]{1,2,0:T(8,128)S(1)}, u32[]{:S(2)}) copy-start(f32[3,1024,1024]{1,2,0:T(8,128)S(1)} %multiply_add_fusion) | copy-start | bytes 37748740
  44.3 52.9 %all-to-all-start = ((bf16[8,128,1024]{2,1,0:T(8,128)(2,1)}), bf16[8,128,1024]{2,1,0:T(8,128)(2,1)}, u32[]{:S(2)}, u32[]{:S(2)}) async-start(bf16[8,128,1024]{2,1,0:T(8,128)(2,1)} %bitcast.6), calls=%async_computation | async-start | bytes 4194304 | tf_op jit(solution)/shard_map/all_to_all | solution.py:70
  49.2 334.5 %all-gather.2.cloned.1.call-start = ((), (), s32[]{:S(2)}) async-start(), calls=%async_computation.2 | async-start | bytes 10485760 | tf_op jit(solution)/shard_map/all_gather | solution.py:83
  50.1 3.4 copy-start.2
  50.2 3.3 copy-start.4
  70.8 89.6 %copy-start.7 = (f32[2048]{0:T(1024)}, f32[2048]{0:T(1024)S(1)}, u32[]{:S(2)}) copy-start(f32[2048]{0:T(1024)S(1)} %get-tuple-element.17) | copy-start | bytes 24580
  181.4 37.7 %slice-start = ((f32[64,2048]{1,0:T(8,128)}), f32[1,2048]{1,0:T(1,128)S(1)}, s32[]{:S(2)}) async-start(f32[64,2048]{1,0:T(8,128)} %multiply_add_fusion.1), calls=%async_computation.3 | async-start | bytes 16384 | tf_op jit(solution)/shard_map/slice | solution.py:50
  210.8 0.7 copy-start.1
  237.2 6.3 %copy-start.8 = (pred[64,64]{1,0:T(8,128)(4,1)S(1)}, pred[64,64]{1,0:T(8,128)(4,1)}, u32[]{:S(2)}) copy-start(pred[64,64]{1,0:T(8,128)(4,1)} %subtract_compare_fusion) | copy-start | bytes 12292
  243.5 4.2 %copy-start.3 = (f32[16,128]{0,1:T(8,128)S(1)}, f32[16,128]{0,1:T(8,128)}, u32[]{:S(2)}) copy-start(f32[16,128]{0,1:T(8,128)} %copy-done.2) | copy-start | bytes 24580
  243.5 4.2 %copy-start.5 = (f32[16,128]{0,1:T(8,128)S(1)}, f32[16,128]{0,1:T(8,128)}, u32[]{:S(2)}) copy-start(f32[16,128]{0,1:T(8,128)} %copy-done.4) | copy-start | bytes 24580
  243.5 4.2 %copy-start.6 = (f32[16,128]{0,1:T(8,128)S(1)}, f32[16,128]{0,1:T(8,128)}, u32[]{:S(2)}) copy-start(f32[16,128]{0,1:T(8,128)} %copy.59) | copy-start | bytes 24580
  313.1 5.4 %copy-start.9 = (f32[1024]{0:T(1024)S(1)}, f32[1024]{0:T(1024)}, u32[]{:S(2)}) copy-start(f32[1024]{0:T(1024)} %param.10) | copy-start | bytes 12292
Sparse Core Ops, SparseCore 0:
  326.3 57.3 all-gather.1
where the time goes:
time: 408 us; the launch traced here: 405 us
  local copies, waits for them, and re-layouts  157 us (38%)
  waiting for transfers between devices  84 us (21%)
  other arithmetic  59.2 us (15%)
  blocking collectives  52 us (13%)
  matrix products  29.6 us (7%)
  between operations  13.7 us (3%)
  starting transfers between devices  9.79 us (2%)
    slice x24, local copies, waits for them, and re-layouts, channel_conv(): _, states = lax.associative_scan(combine, (decays, closing), axis=0)  83.2 us
    all_gather x1, waiting for transfers between devices, shards(): lax.all_gather(gated_mix, 'ch', axis=1, tiled=True)  57.5 us
    all_to_all x1, blocking collectives, shards(): lax.all_to_all(long_part, 'ctx', split_axis=1, concat_axis=0, tiled=True)  52 us
    unnamed x26, local copies, waits for them, and re-layouts  27.2 us
    all_to_all x1, waiting for transfers between devices, shards(): lax.all_to_all(channel_major, 'ctx', split_axis=0, concat_axis=1, tiled=T...  26.5 us
    add x1, other arithmetic, shards(): featured + tap_weights[tap_index].astype(jnp.float32)[:, None, :] * exten...  15.7 us
    gather x2, local copies, waits for them, and re-layouts, make_tables(): kernel[jnp.maximum(offsets, 0)]  15.3 us
    dot_general x1, matrix products, shards(): jnp.dot(lax.all_gather(gated_mix, 'ch', axis=1, tiled=True), out_weight,...  14.7 us
  transfers between devices with their start and end apart: 3, of which 2 were waited for; matrix products, arithmetic and copies ran while one was open for 8% of the time, Pallas kernels for 0%

commit v1 on v0

--- a/solution.py
+++ b/solution.py
@@ -4,6 +4,18 @@
 from jax.sharding import PartitionSpec as P
 
 BLOCK = 64
+
+
+def exchange_directly(array, axis, split, join):
+    ways, here = (lax.axis_size(axis), lax.axis_index(axis))
+    width = array.shape[split] // ways
+    turned = jnp.roll(array, -here * width, axis=split)
+    got = [lax.slice_in_dim(turned, 0, width, axis=split)]
+    for far in range(1, ways):
+        sent = lax.slice_in_dim(turned, far * width, (far + 1) * width, axis=split)
+        got.append(lax.ppermute(sent, axis, [(d, (d + far) % ways) for d in range(ways)]))
+    line = jnp.concatenate(got[::-1], axis=join)
+    return jnp.roll(line, (here + 1) * got[0].shape[join], axis=join)
 
 
 def shifted(value, axis, steps):
@@ -73,7 +85,7 @@
     rates_here = lax.dynamic_slice_in_dim(pole_rates, first_channel, share_width, 1)
     residues_here = lax.dynamic_slice_in_dim(residues, first_channel, share_width, 1)
     long_part = channel_conv(spread, rates_here, residues_here).astype(jnp.bfloat16)
-    returned = lax.all_to_all(long_part, "ctx", split_axis=1, concat_axis=0, tiled=True)
+    returned = exchange_directly(long_part, "ctx", 1, 0)
     long_mix = jnp.transpose(returned)
     gated_mix = featured[0] * (
         long_mix.astype(jnp.float32) + long_bias[None, :] * mixed_input.astype(jnp.float32)

time: 408 us -> 405 us (level)
  blocking collectives: 52 us -> 0 us
  waiting for transfers between devices: 84 us -> 126 us
  starting transfers between devices: 9.79 us -> 17.5 us
    all_to_all x1 -> x0, blocking collectives: 52 us -> none  [shards(): lax.all_to_all(long_part, 'ctx', split_axis=1, concat_axis=0, tiled=True)]
    ppermute x0 -> x7, waiting for transfers between devices: none -> 40 us  [exchange_directly(): lax.ppermute(sent, axis, [(d, (d + far) % ways) for d in range(ways)])]
    ppermute x0 -> x7, starting transfers between devices: none -> 7.68 us  [exchange_directly(): lax.ppermute(sent, axis, [(d, (d + far) % ways) for d in range(ways)])]
    convert_element_type x1 -> x0, local copies, waits for them, and re-layouts: 5.36 us -> none  [shards(): long_mix.astype(jnp.float32)]
    convert_element_type x1 -> x2, local copies, waits for them, and re-layouts: 3.29 us -> 7.4 us  [shards(): channel_conv(spread, rates_here, residues_here).astype(jnp.bfloat16)]
    unnamed x26 -> x41, local copies, waits for them, and re-layouts: 27.2 us -> 27.4 us
  transfers between devices with their start and end apart: 3 -> 10, of which waited for: 2 -> 7; matrix products, arithmetic and copies ran while one was open for 8% -> 8% of each run, Pallas kernels for 0% -> 0%
where the time goes in v1:
time: 405 us; the launch traced here: 402 us
  local copies, waits for them, and re-layouts  157 us (39%)
  waiting for transfers between devices  126 us (31%)
  other arithmetic  58.5 us (14%)
  matrix products  29.6 us (7%)
  starting transfers between devices  17.5 us (4%)
  between operations  13.9 us (3%)
    slice x24, local copies, waits for them, and re-layouts, channel_conv(): _, states = lax.associative_scan(combine, (decays, closing), axis=0)  83.2 us
    all_gather x1, waiting for transfers between devices, shards(): lax.all_gather(gated_mix, 'ch', axis=1, tiled=True)  59.4 us
    ppermute x7, waiting for transfers between devices, exchange_directly(): lax.ppermute(sent, axis, [(d, (d + far) % ways) for d in range(ways)])  40 us
    unnamed x41, local copies, waits for them, and re-layouts  27.4 us
    all_to_all x1, waiting for transfers between devices, shards(): lax.all_to_all(channel_major, 'ctx', split_axis=0, concat_axis=1, tiled=T...  26.5 us
    add x1, other arithmetic, shards(): featured + tap_weights[tap_index].astype(jnp.float32)[:, None, :] * exten...  15.7 us
    gather x2, local copies, waits for them, and re-layouts, make_tables(): kernel[jnp.maximum(offsets, 0)]  15.3 us
    dot_general x1, matrix products, shards(): jnp.dot(lax.all_gather(gated_mix, 'ch', axis=1, tiled=True), out_weight,...  14.7 us
  transfers between devices with their start and end apart: 10, of which 7 were waited for; matrix products, arithmetic and copies ran while one was open for 8% of the time, Pallas kernels for 0%

profile of v1, /device:TPU:0, one launch (start us, length us, event | category | flops | bytes accessed | tf_op | source)
XLA Modules:
  0.0 402.4 jit_solution(9385975646173363368)
XLA Ops:
  7.4 4.9 %collective-permute-start = (bf16[3,2,1024]{2,1,0:T(2,128)(2,1)S(1)}, bf16[3,2,1024]{2,1,0:T(2,128)(2,1)S(1)}, u32[]{:S(2)}, u32[]{:S(2)}) collective-permute-start(bf16[3,2,1024]{2,1,0:T(2,128)(2,1)S(1)} %slice.200), channel_id=1, source_target_pairs={{0,4},{4,8},{8,12},{12,16},{16,20},{20,24},{24,28},{1,5},{5,9},{9,... | collective-permute-start | bytes 36872 | tf_op jit(solution)/shard_map/ppermute | solution.py:24
  13.0 8.6 %copy.44 = bf16[3,1024,1024]{1,2,0:T(8,128)(2,1)} copy(bf16[3,1024,1024]{2,1,0:T(8,128)(2,1)} %param.6) | data formatting | bytes 12582912 | tf_op args[0]
  22.0 15.7 %multiply_add_fusion = f32[3,1024,1024]{1,2,0:T(8,128)S(1)} fusion(bf16[3,1024,1024]{1,2,0:T(8,128)(2,1)} %copy.44, bf16[3,2,1024]{1,2,0:T(8,128)(2,1)S(1)} %copy.45, f32[3,1024]{1,0:T(4,128)S(1)} %get-tuple-element.19, f32[3,1024]{1,0:T(4,128)S(1)} %get-tuple-element.20, f32[3,1024]{1,0:T(4,128)S(1)} %get-tuple-element.18), kind=kLoop, calls=%fused_computation.1 | loop fusion | flops 44040192 | bytes 18923520 | tf_op jit(solution)/shard_map/add | solution.py:77
  37.8 4.5 %copy-done = f32[3,1024,1024]{1,2,0:T(8,128)} copy-done((f32[3,1024,1024]{1,2,0:T(8,128)}, f32[3,1024,1024]{1,2,0:T(8,128)S(1)}, u32[]{:S(2)}) %copy-start) | copy-done | bytes 12582936
  44.3 4.9 %all-to-all-start = ((bf16[8,128,1024]{2,1,0:T(8,128)(2,1)}), bf16[8,128,1024]{2,1,0:T(8,128)(2,1)}, u32[]{:S(2)}, u32[]{:S(2)}) async-start(bf16[8,128,1024]{2,1,0:T(8,128)(2,1)} %bitcast.6), calls=%async_computation | async-start | bytes 4194304 | tf_op jit(solution)/shard_map/all_to_all | solution.py:82
  53.5 10.8 %gather_fusion = f32[4096,128]{1,0:T(8,128)S(1)} fusion(f32[64,128]{1,0:T(8,128)S(1)} %copy.50, s32[4096]{0:T(1024)S(1)} %broadcast_clamp_fusion), kind=kCustom, calls=%fused_computation | custom fusion | bytes 4210688 | tf_op jit(solution)/shard_map/gather | solution.py:36
  64.3 4.6 %copy.51 = f32[64,64,128]{1,0,2:T(8,128)} copy(f32[64,64,128]{2,1,0:T(8,128)S(1)} %bitcast.52) | data formatting | bytes 4194304 | tf_op jit(solution)/shard_map/gather | solution.py:36
  70.8 26.5 %all-to-all-done = bf16[8,128,1024]{2,1,0:T(8,128)(2,1)} async-done(((bf16[8,128,1024]{2,1,0:T(8,128)(2,1)}), bf16[8,128,1024]{2,1,0:T(8,128)(2,1)}, u32[]{:S(2)}, u32[]{:S(2)}) %all-to-all-start) | async-done | bytes 2097184 | tf_op jit(solution)/shard_map/all_to_all | solution.py:82
  97.3 3.9 copy.47
  101.2 3.8 copy.52
  108.0 20.3 %slice.211 = f32[64,2048]{0,1:T(8,128)} slice(f32[128,2048]{0,1:T(8,128)S(1)} %bitcast.48), slice={[0:127:2], [0:2048:1]} | slice | bytes 1048576 | tf_op jit(solution)/shard_map/slice | solution.py:62
  128.2 21.9 %slice.212 = f32[64,2048]{0,1:T(8,128)} slice(f32[128,2048]{0,1:T(8,128)S(1)} %bitcast.49), slice={[1:128:2], [0:2048:1]} | slice | bytes 1048576 | tf_op jit(solution)/shard_map/slice | solution.py:62
  184.4 21.6 %slice.250 = f32[63,2048]{0,1:T(8,128)} slice(f32[128,2048]{0,1:T(8,128)S(1)} %bitcast.50), slice={[2:128:2], [0:2048:1]} | slice | bytes 1032192 | tf_op jit(solution)/shard_map/slice | solution.py:62
  225.5 4.6 %pad.124 = f32[128,2048]{1,0:T(8,128)} pad(f32[64,2048]{1,0:T(8,128)} %add.150, f32[]{:T(128)} %constant.53.clone.1), padding=1_0_1x0_0_0 | pad | bytes 1572868
  243.5 4.2 %fusion.4 = f32[128,128,64]{1,2,0:T(8,128)S(1)} fusion(bf16[128,128,64]{1,2,0:T(8,128)(2,1)S(1)} %copy.52, f32[64,64,128]{1,0,2:T(8,128)} %copy.51, pred[64,64]{1,0:T(8,128)(4,1)S(1)} %copy-done.8), kind=kOutput, calls=%fused_computation.14 | convolution fusion | flops 805830656 | bytes 8392704 | tf_op jit(solution)/shard_map/cij,cnj->cni/dot_general | solution.py:57
  247.7 7.8 %add_convert_fusion = bf16[128,128,64]{1,2,0:T(8,128)(2,1)S(1)} fusion(f32[128,128,64]{1,2,0:T(8,128)S(1)} %fusion.4, f32[128,128,16]{0,2,1:T(8,128)S(1)} %bitcast.55, f32[16,128]{0,1:T(8,128)S(1)} %copy-done.6, f32[16,128]{0,1:T(8,128)S(1)} %copy-done.5, f32[16,128]{0,1:T(8,128)S(1)} %copy-done.3), kind=kOutput, calls=%fused_computation.16 | convolution fusion | flops 203816960 | bytes 7364608 | tf_op jit(solution)/shard_map/ipc,ncp->cni/dot_general | solution.py:65
  258.8 4.1 %copy.62 = bf16[128,8192]{1,0:T(8,128)(2,1)} copy(bf16[128,8192]{0,1:T(8,128)(2,1)} %bitcast.54) | data formatting | bytes 4194304 | tf_op jit(solution)/shard_map/convert_element_type | solution.py:87
  268.7 4.3 %collective-permute-start.4 = (bf16[128,1024]{1,0:T(8,128)(2,1)}, bf16[128,1024]{1,0:T(8,128)(2,1)S(1)}, u32[]{:S(2)}, u32[]{:S(2)}) collective-permute-start(bf16[128,1024]{1,0:T(8,128)(2,1)} %get-tuple-element.10), channel_id=1, source_target_pairs={{0,16},{4,20},{8,24},{12,28},{16,0},{20,4},{24,8},{28,12},{1,17},{... | collective-permute-start | bytes 786440 | tf_op jit(solution)/shard_map/ppermute | solution.py:16
  276.3 5.7 %collective-permute-done.2 = bf16[128,1024]{1,0:T(8,128)(2,1)S(1)} collective-permute-done((bf16[128,1024]{1,0:T(8,128)(2,1)}, bf16[128,1024]{1,0:T(8,128)(2,1)S(1)}, u32[]{:S(2)}, u32[]{:S(2)}) %collective-permute-start.2) | collective-permute-done | bytes 262176 | tf_op jit(solution)/shard_map/ppermute | solution.py:16
  282.0 5.1 %collective-permute-done.3 = bf16[128,1024]{1,0:T(8,128)(2,1)S(1)} collective-permute-done((bf16[128,1024]{1,0:T(8,128)(2,1)}, bf16[128,1024]{1,0:T(8,128)(2,1)S(1)}, u32[]{:S(2)}, u32[]{:S(2)}) %collective-permute-start.3) | collective-permute-done | bytes 262176 | tf_op jit(solution)/shard_map/ppermute | solution.py:16
  287.1 25.9 %collective-permute-done.4 = bf16[128,1024]{1,0:T(8,128)(2,1)S(1)} collective-permute-done((bf16[128,1024]{1,0:T(8,128)(2,1)}, bf16[128,1024]{1,0:T(8,128)(2,1)S(1)}, u32[]{:S(2)}, u32[]{:S(2)}) %collective-permute-start.4) | collective-permute-done | bytes 262176 | tf_op jit(solution)/shard_map/ppermute | solution.py:16
  314.5 6.9 %fusion.3 = bf16[1024,1024]{0,1:T(8,128)(2,1)} fusion(f32[3,1024,1024]{1,2,0:T(8,128)} %copy-done, f32[1024]{0:T(1024)S(1)} %copy-done.9, bf16[2048,1024]{1,0:T(8,128)(2,1)S(1)} %slice_dynamic-update-slice_fusion.1, s32[]{:T(128)S(6)} %select_n.42), kind=kLoop, calls=%fused_computation.10 | loop fusion | flops 8388608 | bytes 16781316 | tf_op jit(solution)/shard_map/convert_element_type | solution.py:93
  321.4 59.4 %all-gather.2.cloned.1.call-done = bf16[1024,4096]{0,1:T(8,128)(2,1)} async-done(((bf16[1024,1024]{0,1:T(8,128)(2,1)}), bf16[1024,4096]{0,1:T(8,128)(2,1)}) %all-gather.2.cloned.1.call-update) | async-done | bytes 8388624 | tf_op jit(solution)/shard_map/all_gather | solution.py:95
  380.8 14.7 %convolution_convert_fusion = bf16[1024,1024]{1,0:T(8,128)(2,1)} fusion(bf16[1024,4096]{0,1:T(8,128)(2,1)} %all-gather.2.cloned.1.call-done, bf16[4096,1024]{1,0:T(8,128)(2,1)} %param.11), kind=kOutput, calls=%fused_computation.21 | convolution fusion | flops 8590983168 | bytes 18874368 | tf_op jit(solution)/shard_map/dot_general | solution.py:94
  (137 shorter events, 93.8 us)
Async XLA Ops:
  7.4 14.2 %collective-permute-start = (bf16[3,2,1024]{2,1,0:T(2,128)(2,1)S(1)}, bf16[3,2,1024]{2,1,0:T(2,128)(2,1)S(1)}, u32[]{:S(2)}, u32[]{:S(2)}) collective-permute-start(bf16[3,2,1024]{2,1,0:T(2,128)(2,1)S(1)} %slice.200), channel_id=1, source_target_pairs={{0,4},{4,8},{8,12},{12,16},{16,20},{20,24},{24,28},{1,5},{5,9},{9,... | collective-permute-start | bytes 36872 | tf_op jit(solution)/shard_map/ppermute | solution.py:24
  37.8 4.5 %copy-start = (f32[3,1024,1024]{1,2,0:T(8,128)}, f32[3,1024,1024]{1,2,0:T(8,128)S(1)}, u32[]{:S(2)}) copy-start(f32[3,1024,1024]{1,2,0:T(8,128)S(1)} %multiply_add_fusion) | copy-start | bytes 37748740
  44.3 52.9 %all-to-all-start = ((bf16[8,128,1024]{2,1,0:T(8,128)(2,1)}), bf16[8,128,1024]{2,1,0:T(8,128)(2,1)}, u32[]{:S(2)}, u32[]{:S(2)}) async-start(bf16[8,128,1024]{2,1,0:T(8,128)(2,1)} %bitcast.6), calls=%async_computation | async-start | bytes 4194304 | tf_op jit(solution)/shard_map/all_to_all | solution.py:82
  49.2 331.6 %all-gather.2.cloned.1.call-start = ((), (), s32[]{:S(2)}) async-start(), calls=%async_computation.1 | async-start | bytes 10485760 | tf_op jit(solution)/shard_map/all_gather | solution.py:95
  50.1 3.4 copy-start.2
  50.2 3.3 copy-start.4
  70.8 89.5 %copy-start.7 = (f32[2048]{0:T(1024)}, f32[2048]{0:T(1024)S(1)}, u32[]{:S(2)}) copy-start(f32[2048]{0:T(1024)S(1)} %get-tuple-element.24) | copy-start | bytes 24580
  181.4 37.7 %slice-start = ((f32[64,2048]{1,0:T(8,128)}), f32[1,2048]{1,0:T(1,128)S(1)}, s32[]{:S(2)}) async-start(f32[64,2048]{1,0:T(8,128)} %multiply_add_fusion.1), calls=%async_computation.2 | async-start | bytes 16384 | tf_op jit(solution)/shard_map/slice | solution.py:62
  210.8 0.7 copy-start.1
  237.1 6.3 %copy-start.8 = (pred[64,64]{1,0:T(8,128)(4,1)S(1)}, pred[64,64]{1,0:T(8,128)(4,1)}, u32[]{:S(2)}) copy-start(pred[64,64]{1,0:T(8,128)(4,1)} %subtract_compare_fusion) | copy-start | bytes 12292
  243.4 4.2 %copy-start.3 = (f32[16,128]{0,1:T(8,128)S(1)}, f32[16,128]{0,1:T(8,128)}, u32[]{:S(2)}) copy-start(f32[16,128]{0,1:T(8,128)} %copy-done.2) | copy-start | bytes 24580
  243.5 4.2 %copy-start.5 = (f32[16,128]{0,1:T(8,128)S(1)}, f32[16,128]{0,1:T(8,128)}, u32[]{:S(2)}) copy-start(f32[16,128]{0,1:T(8,128)} %copy-done.4) | copy-start | bytes 24580
  243.5 4.2 %copy-start.6 = (f32[16,128]{0,1:T(8,128)S(1)}, f32[16,128]{0,1:T(8,128)}, u32[]{:S(2)}) copy-start(f32[16,128]{0,1:T(8,128)} %copy.60) | copy-start | bytes 24580
  266.4 9.5 %collective-permute-start.1 = (bf16[128,1024]{1,0:T(8,128)(2,1)}, bf16[128,1024]{1,0:T(8,128)(2,1)S(1)}, u32[]{:S(2)}, u32[]{:S(2)}) collective-permute-start(bf16[128,1024]{1,0:T(8,128)(2,1)} %get-tuple-element.13), channel_id=1, source_target_pairs={{0,28},{4,0},{8,4},{12,8},{16,12},{20,16},{24,20},{28,24},{1,29},{... | collective-permute-start | bytes 786440 | tf_op jit(solution)/shard_map/ppermute | solution.py:16
  268.7 13.2 %collective-permute-start.2 = (bf16[128,1024]{1,0:T(8,128)(2,1)}, bf16[128,1024]{1,0:T(8,128)(2,1)S(1)}, u32[]{:S(2)}, u32[]{:S(2)}) collective-permute-start(bf16[128,1024]{1,0:T(8,128)(2,1)} %get-tuple-element.12), channel_id=1, source_target_pairs={{0,24},{4,28},{8,0},{12,4},{16,8},{20,12},{24,16},{28,20},{1,25},{... | collective-permute-start | bytes 786440 | tf_op jit(solution)/shard_map/ppermute | solution.py:16
  268.7 18.4 %collective-permute-start.3 = (bf16[128,1024]{1,0:T(8,128)(2,1)}, bf16[128,1024]{1,0:T(8,128)(2,1)S(1)}, u32[]{:S(2)}, u32[]{:S(2)}) collective-permute-start(bf16[128,1024]{1,0:T(8,128)(2,1)} %get-tuple-element.11), channel_id=1, source_target_pairs={{0,20},{4,24},{8,28},{12,0},{16,4},{20,8},{24,12},{28,16},{1,21},{... | collective-permute-start | bytes 786440 | tf_op jit(solution)/shard_map/ppermute | solution.py:16
  268.7 44.3 %collective-permute-start.4 = (bf16[128,1024]{1,0:T(8,128)(2,1)}, bf16[128,1024]{1,0:T(8,128)(2,1)S(1)}, u32[]{:S(2)}, u32[]{:S(2)}) collective-permute-start(bf16[128,1024]{1,0:T(8,128)(2,1)} %get-tuple-element.10), channel_id=1, source_target_pairs={{0,16},{4,20},{8,24},{12,28},{16,0},{20,4},{24,8},{28,12},{1,17},{... | collective-permute-start | bytes 786440 | tf_op jit(solution)/shard_map/ppermute | solution.py:16
  273.0 41.1 %collective-permute-start.5 = (bf16[128,1024]{1,0:T(8,128)(2,1)}, bf16[128,1024]{1,0:T(8,128)(2,1)S(1)}, u32[]{:S(2)}, u32[]{:S(2)}) collective-permute-start(bf16[128,1024]{1,0:T(8,128)(2,1)} %get-tuple-element.9), channel_id=1, source_target_pairs={{0,12},{4,16},{8,20},{12,24},{16,28},{20,0},{24,4},{28,8},{1,13},{... | collective-permute-start | bytes 786440 | tf_op jit(solution)/shard_map/ppermute | solution.py:16
  275.8 38.7 %copy-start.9 = (f32[1024]{0:T(1024)S(1)}, f32[1024]{0:T(1024)}, u32[]{:S(2)}) copy-start(f32[1024]{0:T(1024)} %param.10) | copy-start | bytes 12292
  275.8 38.3 %collective-permute-start.6 = (bf16[128,1024]{1,0:T(8,128)(2,1)S(1)}, bf16[128,1024]{1,0:T(8,128)(2,1)S(1)}, u32[]{:S(2)}, u32[]{:S(2)}) collective-permute-start(bf16[128,1024]{1,0:T(8,128)(2,1)S(1)} %get-tuple-element.8), channel_id=1, source_target_pairs={{0,8},{4,12},{8,16},{12,20},{16,24},{20,28},{24,0},{28,4},{1,9},{5... | collective-permute-start | bytes 786440 | tf_op jit(solution)/shard_map/ppermute | solution.py:16
  282.0 32.2 %collective-permute-start.7 = (bf16[128,1024]{1,0:T(8,128)(2,1)S(1)}, bf16[128,1024]{1,0:T(8,128)(2,1)S(1)}, u32[]{:S(2)}, u32[]{:S(2)}) collective-permute-start(bf16[128,1024]{1,0:T(8,128)(2,1)S(1)} %get-tuple-element.7), channel_id=1, source_target_pairs={{0,4},{4,8},{8,12},{12,16},{16,20},{20,24},{24,28},{28,0},{1,5},{5... | collective-permute-start | bytes 786440 | tf_op jit(solution)/shard_map/ppermute | solution.py:16
Sparse Core Ops, SparseCore 0:
  321.5 59.2 all-gather.1
